TPU v7x, 256 devices: a whole 4x4x8 slice. The times are simulated.
256 devices in a mesh: seq: 64 (over y, z, core), tr: 2 (over x_lo), tc: 2 (over x_hi).
Axes of the slice: x: 4 (x_hi: 2, x_lo: 2; x = x_hi * 2 + x_lo), y: 4, z: 8, core: 2. Of those that a mesh axis runs over, the one named last changes fastest.
Arguments:
- activations: bfloat16 [65536, 1024], P('seq', ('tr', 'tc')), may hold values from -6 to 6
- seg_len: int32 [64], P('seq'), may hold values from 1 to 1024, as said below
- seg_start: int32 [64], P('seq'), may hold values from 0 to 1, as said below
- memory_rates: float32 [3, 64, 8], P(None, 'seq'), may hold values from 0 to 1, as said below
- w_qkv: bfloat16 [1024, 3, 1024], P(None, None, ('tr', 'tc')), may hold values from -0.1875 to 0.1875
- conv_w: float32 [4, 3, 1024], P(None, None, ('tr', 'tc')), may hold values from -3 to 3
- persistent: bfloat16 [2, 16, 1024], P(None, None, ('tr', 'tc')), may hold values from -6 to 6
- w_out: bfloat16 [1024, 1024], P(('tr', 'tc')), may hold values from -0.1875 to 0.1875
- w_gate: bfloat16 [1024, 2816], P(None, ('tr', 'tc')), may hold values from -0.1875 to 0.1875
- w_up: bfloat16 [1024, 2816], P(None, ('tr', 'tc')), may hold values from -0.1875 to 0.1875
- w_down: bfloat16 [2816, 1024], P(('tr', 'tc')), may hold values from -0.109375 to 0.109375
Outputs:
- layer_out: bfloat16 [65536, 1024], P('seq', ('tr', 'tc'))
Inputs may be any that keep to these rules, and one draw needn't show every extreme that they name: `seg_start`: 1 where a segment begins a prompt, 0 where it continues the prompt of the segment before; segment 0 begins a prompt; a prompt spans at most 32 segments, and in every draw one prompt spans exactly that many. `seg_len`: live tokens at the head of each segment; every segment of a prompt but its last is full. `memory_rates`: all three tables lie strictly between 0 and 1.
All inputs are finite; a program needn't handle non-finite values.
Results may differ from a plain program's by a relative error of at most 0.015.
Values may be sent and summed in bfloat16 or wider, within the bound.
No kernel may reach another device: no remote copies, remote signals or barrier semaphores. Data moves between devices by JAX's collectives and lax.ppermute only.
A program may use at most 192 MiB of HBM per device.

v0:
```python
import jax
import jax.numpy as jnp
from jax import lax
from jax.sharding import PartitionSpec as P

HD = 128
SEG = 1024
CONV = 4
PROMPT_SPAN = 32


epsilon = 1e-06
score_scale = 8.0


def passed_along(block, axis, distance):
    devices = range(lax.axis_size(axis))
    route = [(i - distance, i) for i in devices if i - distance in devices]
    return lax.ppermute(block, axis, route)


def exact_pair(block):
    high = block.astype(jnp.bfloat16)
    low = (block - high.astype(jnp.float32)).astype(jnp.bfloat16)
    return jnp.concatenate([high, low], -1)


def from_pair(pair):
    half = pair.shape[-1] // 2
    return pair[..., :half].astype(jnp.float32) + pair[..., half:].astype(jnp.float32)


def memory_entering(seg_map, seg_shift, axis, reach):
    if reach < 2:
        return jnp.zeros_like(seg_shift[:, : seg_shift.shape[-1]])
    distance = 1
    while 2 * distance < reach:
        payload = jnp.concatenate([seg_map.astype(jnp.bfloat16), exact_pair(seg_shift)], -1)
        arrived = passed_along(payload, axis, distance)
        width = seg_map.shape[-1]
        shift_before = from_pair(arrived[..., width:])
        map_before = arrived[..., :width].astype(jnp.float32)
        seg_shift = exact_product(seg_map, shift_before) + seg_shift
        seg_map = exact_product(seg_map, map_before)
        distance *= 2
    rows = seg_shift.shape[-1]
    last = jnp.concatenate(
        [seg_map[:, :rows].astype(jnp.bfloat16), exact_pair(seg_shift[:, :rows])], -1
    )
    last = passed_along(last, axis, 1)
    width = seg_map.shape[-1]
    earlier = from_pair(passed_along(exact_pair(seg_shift), axis, distance + 1))
    near_map = last[..., :width].astype(jnp.float32)
    return exact_product(near_map, earlier) + from_pair(last[..., width:])


def group_route(axis, distance):
    count = lax.axis_size(axis)
    return [(i, (i + distance) % count) for i in range(count)]


def gathered_products(local, weights, axis):
    count, index = (lax.axis_size(axis), lax.axis_index(axis))
    width = local.shape[1]
    pieces = [(local, index)]
    for distance in range(1, count):
        arrived = lax.ppermute(local, axis, group_route(axis, distance))
        pieces.append((arrived, (index - distance) % count))
    totals = [None] * len(weights)
    squares = None
    for piece, source in pieces:
        piece_f = piece.astype(jnp.float32)
        part_sq = jnp.sum(piece_f * piece_f, -1)
        squares = part_sq if squares is None else squares + part_sq
        for k, weight in enumerate(weights):
            rows = lax.dynamic_slice_in_dim(weight, source * width, width, 0)
            term = jnp.dot(piece, rows, preferred_element_type=jnp.float32)
            totals[k] = term if totals[k] is None else totals[k] + term
    return totals, squares


def scattered_sum(left, weight, axis):
    count, index = (lax.axis_size(axis), lax.axis_index(axis))
    width = weight.shape[1] // count

    def block(owner):
        cols = lax.dynamic_slice_in_dim(weight, owner * width, width, 1)
        return jnp.dot(left, cols, preferred_element_type=jnp.float32).astype(jnp.bfloat16)

    total = None
    for distance in range(1, count):
        arrived = lax.ppermute(block((index + distance) % count), axis, group_route(axis, distance))
        total = arrived.astype(jnp.float32) if total is None else total + arrived.astype(jnp.float32)
    own = block(index).astype(jnp.float32)
    return own if total is None else total + own


def unit_rows(values_in):
    return values_in * lax.rsqrt(jnp.sum(values_in * values_in, -1, keepdims=True) + epsilon)


def exact_product(left, right):
    return jnp.matmul(left, right, precision=lax.Precision.HIGHEST)


def body(
    activations,
    seg_len,
    seg_start,
    memory_rates,
    w_qkv,
    conv_w,
    persistent,
    w_out,
    w_gate,
    w_up,
    w_down,
):
    token_rows, local_feat = activations.shape
    seg_count = seg_len.shape[0]
    full_width = w_qkv.shape[0]
    head_width = w_qkv.shape[2]
    local_heads = head_width // HD
    group_index = lax.axis_index(("tr", "tc"))
    wide = w_qkv.reshape(full_width, 3 * head_width)
    row_ids = jnp.arange(token_rows, dtype=jnp.int32)
    position = row_ids % SEG
    segment_of = row_ids // SEG
    continuing = seg_start[segment_of] == 0
    (projected,), squares = gathered_products(activations, (wide,), ("tr", "tc"))
    qkv = (projected * lax.rsqrt(squares / full_width + epsilon)[:, None]).astype(jnp.bfloat16)
    edge_rows = passed_along(qkv[token_rows - (CONV - 1) :], "seq", 1)
    extended = jnp.concatenate([edge_rows, qkv], 0)
    taps = conv_w.reshape(CONV, 3 * head_width)
    convolved = jnp.zeros((token_rows, 3 * head_width), jnp.float32)
    for offset in range(CONV):
        shifted = extended[CONV - 1 - offset : CONV - 1 - offset + token_rows].astype(jnp.float32)
        valid = (position >= offset) | continuing
        convolved = convolved + jnp.where(valid[:, None], taps[offset] * shifted, 0.0)
    parts = convolved.reshape(token_rows, 3, local_heads, HD)
    query_n = unit_rows(parts[:, 0]).astype(jnp.bfloat16)
    key_n = unit_rows(parts[:, 1]).astype(jnp.bfloat16)
    value_n = parts[:, 2].astype(jnp.bfloat16)
    pkeys = unit_rows(persistent[0].astype(jnp.float32).reshape(-1, local_heads, HD)).astype(
        jnp.bfloat16
    )
    pvalues = persistent[1].reshape(-1, local_heads, HD)
    persist_rows = pkeys.shape[0]
    live = position < seg_len[segment_of]
    keys_live = jnp.where(live[:, None, None], key_n, jnp.zeros((), jnp.bfloat16)).reshape(
        seg_count, SEG, local_heads, HD
    )
    value_segs = value_n.reshape(seg_count, SEG, local_heads, HD)
    a_mats = jnp.einsum("cthi,cthj->chij", keys_live, keys_live, preferred_element_type=jnp.float32)
    b_mats = jnp.einsum(
        "cthi,cthj->chij", keys_live, value_segs, preferred_element_type=jnp.float32
    )
    my_rates = lax.dynamic_slice_in_dim(memory_rates, group_index * local_heads, local_heads, 2)
    decay_factor = my_rates[0][:, :, None, None]
    eta = my_rates[1][:, :, None, None]
    theta = my_rates[2][:, :, None, None]
    keep = (1 - seg_start).astype(jnp.float32)[:, None, None, None]
    identity = jnp.eye(HD, dtype=jnp.float32)
    upper = jnp.concatenate([(1.0 - decay_factor) * identity - theta * a_mats, eta * identity], -1)
    lower = jnp.concatenate([-theta * a_mats, eta * identity], -1)
    seg_maps = jnp.concatenate([upper, lower], -2) * keep
    seg_shifts = jnp.concatenate([theta * b_mats, theta * b_mats], -2)
    reach = min(PROMPT_SPAN, lax.axis_size("seq"))
    memory_in = memory_entering(seg_maps[0], seg_shifts[0], "seq", reach) * keep[0]
    query_seg = query_n.astype(jnp.float32)
    retr_parts = jnp.einsum("thi,hij->thj", query_seg, memory_in, precision=lax.Precision.HIGHEST)
    mem = retr_parts * lax.rsqrt(jnp.mean(retr_parts * retr_parts, -1, keepdims=True) + epsilon)
    block_rows = min(512, SEG)
    attn_parts = []
    seg_index = 0
    first = seg_index * SEG
    keys_all = jnp.concatenate([pkeys, key_n], 0)
    values_all = jnp.concatenate([pvalues, value_n], 0)
    cols_k = jnp.arange(persist_rows + SEG, dtype=jnp.int32)[None, :] - persist_rows
    for block_start in range(0, SEG, block_rows):
        query_blk = query_n[first + block_start : first + block_start + block_rows]
        scores = score_scale * jnp.einsum(
            "qhd,khd->hqk", query_blk, keys_all, preferred_element_type=jnp.float32
        )
        rows_q = block_start + jnp.arange(block_rows, dtype=jnp.int32)[:, None]
        allow = (cols_k < 0) | (cols_k <= rows_q) & (cols_k < seg_len[seg_index])
        weights = jnp.where(allow[None], jnp.exp(scores), 0.0)
        probs = (weights / jnp.sum(weights, -1, keepdims=True)).astype(jnp.bfloat16)
        attn_parts.append(
            jnp.einsum("hqk,khd->qhd", probs, values_all, preferred_element_type=jnp.float32)
        )
    attn = jnp.concatenate(attn_parts, 0)
    heads_out = (attn + mem).astype(jnp.bfloat16).reshape(token_rows, head_width)
    share = scattered_sum(heads_out, w_out, ("tr", "tc"))
    resid = (activations.astype(jnp.float32) + share).astype(jnp.bfloat16)
    (gate, up_proj), squares2 = gathered_products(resid, (w_gate, w_up), ("tr", "tc"))
    inv_rms2 = lax.rsqrt(squares2 / full_width + epsilon)[:, None]
    hidden = (jax.nn.silu(gate * inv_rms2) * (up_proj * inv_rms2)).astype(jnp.bfloat16)
    ffn_share = scattered_sum(hidden, w_down, ("tr", "tc"))
    return (resid.astype(jnp.float32) + ffn_share).astype(jnp.bfloat16)


def solution(mesh):
    return jax.shard_map(
        body,
        mesh=mesh,
        in_specs=(
            P("seq", ("tr", "tc")),
            P("seq"),
            P("seq"),
            P(None, "seq", None),
            P(None, None, ("tr", "tc")),
            P(None, None, ("tr", "tc")),
            P(None, None, ("tr", "tc")),
            P(("tr", "tc"), None),
            P(None, ("tr", "tc")),
            P(None, ("tr", "tc")),
            P(("tr", "tc"), None),
        ),
        out_specs=P("seq", ("tr", "tc")),
        check_vma=False,
    )
```

profile of v0, /device:TPU:14, one launch (start us, length us, event | category | flops | bytes accessed | tf_op | source)
XLA Modules:
  0.0 275.2 jit_solution(14347631281366291479)
XLA Ops:
  0.5 3.1 %collective-permute-start.2 = (bf16[1024,256]{1,0:T(8,128)(2,1)}, bf16[1024,256]{1,0:T(8,128)(2,1)}, u32[]{:S(2)}, u32[]{:S(2)}) collective-permute-start(bf16[1024,256]{1,0:T(8,128)(2,1)} %param.11), channel_id=1, source_target_pairs={{0,3},{1,0},{2,1},{3,2},{4,7},{5,4},{6,5},{7,6},{8,11},{9,8},{10,9... | collective-permute-start | bytes 1572872 | tf_op jit(solution)/shard_map/ppermute | solution.py:67
  15.2 2.3 fusion.36
  21.0 2.2 collective-permute-done
  24.5 2.2 collective-permute-done.2
  35.7 1.9 collective-permute-start.3
  39.5 6.8 %collective-permute-done.3 = bf16[3,768]{0,1:T(8,128)(2,1)S(1)} collective-permute-done((bf16[3,768]{0,1:T(8,128)(2,1)S(1)}, bf16[3,768]{0,1:T(8,128)(2,1)S(1)}, u32[]{:S(2)}, u32[]{:S(2)}) %collective-permute-start.3) | collective-permute-done | bytes 4640 | tf_op jit(solution)/shard_map/ppermute | solution.py:19
  46.3 3.0 %select_add_fusion = f32[1024,768]{0,1:T(8,128)S(1)} fusion(bf16[1024,768]{0,1:T(8,128)(2,1)S(1)} %fusion.12, bf16[3,768]{0,1:T(8,128)(2,1)S(1)} %collective-permute-done.3, f32[768]{0:T(1024)S(1)} %mul.319, f32[768]{0:T(1024)S(1)} %mul.316, f32[768]{0:T(1024)S(1)} %mul.313, f32[768]{0:T(1024)S(1)} %mul.298, pred[1024]{0:T(1024)(128)(4,1)S(1)} %copy-done.26, ...), kind=kLoop, calls=%fused_computation.8 | loop fusion | flops 18874368 | bytes 4739584 | tf_op jit(solution)/shard_map/add | solution.py:139
  55.4 1.9 collective-permute-start.4
  57.4 10.6 %collective-permute-done.4 = bf16[2,256,512]{1,2,0:T(8,128)(2,1)S(1)} collective-permute-done((bf16[2,256,512]{1,2,0:T(8,128)(2,1)S(1)}, bf16[2,256,512]{1,2,0:T(8,128)(2,1)S(1)}, u32[]{:S(2)}, u32[]{:S(2)}) %collective-permute-start.4) | collective-permute-done | bytes 524320 | tf_op jit(solution)/shard_map/ppermute | solution.py:19
  69.8 2.1 collective-permute-start.5
  71.9 2.0 fusion.7
  75.5 8.3 %collective-permute-done.5 = bf16[2,256,512]{1,2,0:T(8,128)(2,1)} collective-permute-done((bf16[2,256,512]{1,2,0:T(8,128)(2,1)}, bf16[2,256,512]{1,2,0:T(8,128)(2,1)}, u32[]{:S(2)}, u32[]{:S(2)}) %collective-permute-start.5) | collective-permute-done | bytes 524320 | tf_op jit(solution)/shard_map/ppermute | solution.py:19
  86.7 1.9 collective-permute-start.6
  89.3 22.4 %collective-permute-done.6 = bf16[2,256,512]{1,2,0:T(8,128)(2,1)S(1)} collective-permute-done((bf16[2,256,512]{1,2,0:T(8,128)(2,1)S(1)}, bf16[2,256,512]{1,2,0:T(8,128)(2,1)S(1)}, u32[]{:S(2)}, u32[]{:S(2)}) %collective-permute-start.6) | collective-permute-done | bytes 524320 | tf_op jit(solution)/shard_map/ppermute | solution.py:19
  114.6 2.9 %fusion.3 = f32[2,512,1040]{1,2,0:T(8,128)} fusion(pred[512,1040]{0,1:T(8,128)(4,1)S(1)} %copy-done.7, bf16[1024,2,128]{2,0,1:T(8,128)(2,1)S(1)} %copy-done.9, bf16[16,2,128]{2,0,1:T(8,128)(2,1)S(1)} %fusion.114, bf16[1024,2,128]{2,0,1:T(8,128)(2,1)S(1)} %fusion.27), kind=kOutput, calls=%fused_computation.5 | convolution fusion | flops 275824640 | bytes 5586944 | tf_op jit(solution)/shard_map/qhd,khd->hqk/dot_general | solution.py:182
  117.6 3.0 %fusion.1 = f32[2,512,1040]{1,2,0:T(8,128)} fusion(pred[512,1040]{0,1:T(8,128)(4,1)S(1)} %copy-done.6, bf16[1024,2,128]{2,0,1:T(8,128)(2,1)S(1)} %copy-done.9, bf16[16,2,128]{2,0,1:T(8,128)(2,1)S(1)} %fusion.114, bf16[1024,2,128]{2,0,1:T(8,128)(2,1)S(1)} %fusion.27), kind=kOutput, calls=%fused_computation.3 | convolution fusion | flops 275824640 | bytes 5586944 | tf_op jit(solution)/shard_map/qhd,khd->hqk/dot_general | solution.py:182
  120.6 13.3 %collective-permute-done.7 = bf16[2,256,512]{1,2,0:T(8,128)(2,1)S(1)} collective-permute-done((bf16[2,256,512]{1,2,0:T(8,128)(2,1)S(1)}, bf16[2,256,512]{1,2,0:T(8,128)(2,1)S(1)}, u32[]{:S(2)}, u32[]{:S(2)}) %collective-permute-start.7) | collective-permute-done | bytes 524320 | tf_op jit(solution)/shard_map/ppermute | solution.py:19
  138.2 12.7 %collective-permute-start.9 = (bf16[2,256,256]{1,2,0:T(8,128)(2,1)}, bf16[2,256,256]{1,2,0:T(8,128)(2,1)}, u32[]{:S(2)}, u32[]{:S(2)}) collective-permute-start(bf16[2,256,256]{1,2,0:T(8,128)(2,1)} %pad_maximum_fusion.14), channel_id=1, source_target_pairs={{0,68},{4,72},{8,76},{12,80},{16,84},{20,88},{24,92},{28,96},{32,1... | collective-permute-start | bytes 786440 | tf_op jit(solution)/shard_map/ppermute | solution.py:19
  150.9 4.4 %fusion.15 = f32[512,2,128]{0,2,1:T(8,128)S(1)} fusion(f32[2,512,1040]{1,2,0:T(8,128)} %fusion.3, bf16[1024,2,128]{2,0,1:T(8,128)(2,1)S(1)} %bitcast.104, bf16[16,2,128]{2,0,1:T(8,128)(2,1)S(1)} %copy-done.23), kind=kOutput, calls=%fused_computation.42 | convolution fusion | flops 275826688 | bytes 5316608 | tf_op jit(solution)/shard_map/hqk,khd->qhd/dot_general | solution.py:190
  155.3 4.3 %fusion.16 = f32[512,2,128]{0,2,1:T(8,128)S(1)} fusion(f32[2,512,1040]{1,2,0:T(8,128)} %fusion.1, bf16[1024,2,128]{2,0,1:T(8,128)(2,1)S(1)} %bitcast.105, bf16[16,2,128]{2,0,1:T(8,128)(2,1)S(1)} %copy-done.23), kind=kOutput, calls=%fused_computation.43 | convolution fusion | flops 275826688 | bytes 5316608 | tf_op jit(solution)/shard_map/hqk,khd->qhd/dot_general | solution.py:190
  163.1 2.6 collective-permute-start.10
  165.6 23.9 %collective-permute-start.11 = (bf16[1024,256]{1,0:T(8,128)(2,1)S(1)}, bf16[1024,256]{1,0:T(8,128)(2,1)S(1)}, u32[]{:S(2)}, u32[]{:S(2)}) collective-permute-start(bf16[1024,256]{1,0:T(8,128)(2,1)S(1)} %convolution_convert_fusion.2), channel_id=1, source_target_pairs={{0,2},{1,3},{2,0},{3,1},{4,6},{5,7},{6,4},{7,5},{8,10},{9,11},{10,... | collective-permute-start | bytes 1572872 | tf_op jit(solution)/shard_map/ppermute | solution.py:92
  189.6 4.0 %collective-permute-start.12 = (bf16[1024,256]{1,0:T(8,128)(2,1)S(1)}, bf16[1024,256]{1,0:T(8,128)(2,1)S(1)}, u32[]{:S(2)}, u32[]{:S(2)}) collective-permute-start(bf16[1024,256]{1,0:T(8,128)(2,1)S(1)} %convolution_convert_fusion.1), channel_id=1, source_target_pairs={{0,3},{1,0},{2,1},{3,2},{4,7},{5,4},{6,5},{7,6},{8,11},{9,8},{10,9... | collective-permute-start | bytes 1572872 | tf_op jit(solution)/shard_map/ppermute | solution.py:92
  193.6 8.7 %collective-permute-done.11 = bf16[1024,256]{1,0:T(8,128)(2,1)S(1)} collective-permute-done((bf16[1024,256]{1,0:T(8,128)(2,1)S(1)}, bf16[1024,256]{1,0:T(8,128)(2,1)S(1)}, u32[]{:S(2)}, u32[]{:S(2)}) %collective-permute-start.11) | collective-permute-done | bytes 524320 | tf_op jit(solution)/shard_map/ppermute | solution.py:92
  202.3 9.0 %collective-permute-done.12 = bf16[1024,256]{1,0:T(8,128)(2,1)S(1)} collective-permute-done((bf16[1024,256]{1,0:T(8,128)(2,1)S(1)}, bf16[1024,256]{1,0:T(8,128)(2,1)S(1)}, u32[]{:S(2)}, u32[]{:S(2)}) %collective-permute-start.12) | collective-permute-done | bytes 524320 | tf_op jit(solution)/shard_map/ppermute | solution.py:92
  211.9 4.6 %collective-permute-start.15 = (bf16[1024,256]{1,0:T(8,128)(2,1)S(1)}, bf16[1024,256]{1,0:T(8,128)(2,1)S(1)}, u32[]{:S(2)}, u32[]{:S(2)}) collective-permute-start(bf16[1024,256]{1,0:T(8,128)(2,1)S(1)} %get-tuple-element.46), channel_id=1, source_target_pairs={{0,3},{1,0},{2,1},{3,2},{4,7},{5,4},{6,5},{7,6},{8,11},{9,8},{10,9... | collective-permute-start | bytes 1572872 | tf_op jit(solution)/shard_map/ppermute | solution.py:67
  216.5 2.0 collective-permute-start.13
  219.7 9.2 %collective-permute-done.15 = bf16[1024,256]{1,0:T(8,128)(2,1)S(1)} collective-permute-done((bf16[1024,256]{1,0:T(8,128)(2,1)S(1)}, bf16[1024,256]{1,0:T(8,128)(2,1)S(1)}, u32[]{:S(2)}, u32[]{:S(2)}) %collective-permute-start.15) | collective-permute-done | bytes 524320 | tf_op jit(solution)/shard_map/ppermute | solution.py:67
  229.1 10.1 %collective-permute-done.14 = bf16[1024,256]{1,0:T(8,128)(2,1)S(1)} collective-permute-done((bf16[1024,256]{1,0:T(8,128)(2,1)S(1)}, bf16[1024,256]{1,0:T(8,128)(2,1)S(1)}, u32[]{:S(2)}, u32[]{:S(2)}) %collective-permute-start.14) | collective-permute-done | bytes 524320 | tf_op jit(solution)/shard_map/ppermute | solution.py:67
  249.1 4.0 %collective-permute-start.18 = (bf16[1024,256]{1,0:T(8,128)(2,1)S(1)}, bf16[1024,256]{1,0:T(8,128)(2,1)S(1)}, u32[]{:S(2)}, u32[]{:S(2)}) collective-permute-start(bf16[1024,256]{1,0:T(8,128)(2,1)S(1)} %convolution_convert_fusion.5), channel_id=1, source_target_pairs={{0,3},{1,0},{2,1},{3,2},{4,7},{5,4},{6,5},{7,6},{8,11},{9,8},{10,9... | collective-permute-start | bytes 1572872 | tf_op jit(solution)/shard_map/ppermute | solution.py:92
  253.1 11.1 %collective-permute-done.16 = bf16[1024,256]{1,0:T(8,128)(2,1)S(1)} collective-permute-done((bf16[1024,256]{1,0:T(8,128)(2,1)S(1)}, bf16[1024,256]{1,0:T(8,128)(2,1)S(1)}, u32[]{:S(2)}, u32[]{:S(2)}) %collective-permute-start.16) | collective-permute-done | bytes 524320 | tf_op jit(solution)/shard_map/ppermute | solution.py:92
  264.2 9.4 %collective-permute-done.18 = bf16[1024,256]{1,0:T(8,128)(2,1)S(1)} collective-permute-done((bf16[1024,256]{1,0:T(8,128)(2,1)S(1)}, bf16[1024,256]{1,0:T(8,128)(2,1)S(1)}, u32[]{:S(2)}, u32[]{:S(2)}) %collective-permute-start.18) | collective-permute-done | bytes 524320 | tf_op jit(solution)/shard_map/ppermute | solution.py:92
  (169 shorter events, 63.1 us)
Async XLA Ops:
  0.0 219.1 %copy-start = (bf16[1024,704]{0,1:T(8,128)(2,1)S(1)}, bf16[1024,704]{0,1:T(8,128)(2,1)}, u32[]{:S(2)}) copy-start(bf16[1024,704]{0,1:T(8,128)(2,1)} %param.19) | copy-start | bytes 4325380
  0.0 15.2 %copy-start.3 = (bf16[1024,256]{1,0:T(8,128)(2,1)S(1)}, bf16[1024,256]{1,0:T(8,128)(2,1)}, u32[]{:S(2)}) copy-start(bf16[1024,256]{1,0:T(8,128)(2,1)} %param.11) | copy-start | bytes 1572868
  0.0 23.2 %collective-permute-start = (bf16[1024,256]{1,0:T(8,128)(2,1)}, bf16[1024,256]{1,0:T(8,128)(2,1)}, u32[]{:S(2)}, u32[]{:S(2)}) collective-permute-start(bf16[1024,256]{1,0:T(8,128)(2,1)} %param.11), channel_id=1, source_target_pairs={{0,1},{1,2},{2,3},{3,0},{4,5},{5,6},{6,7},{7,4},{8,9},{9,10},{10,1... | collective-permute-start | bytes 1572872 | tf_op jit(solution)/shard_map/ppermute | solution.py:67
  0.5 26.2 %collective-permute-start.2 = (bf16[1024,256]{1,0:T(8,128)(2,1)}, bf16[1024,256]{1,0:T(8,128)(2,1)}, u32[]{:S(2)}, u32[]{:S(2)}) collective-permute-start(bf16[1024,256]{1,0:T(8,128)(2,1)} %param.11), channel_id=1, source_target_pairs={{0,3},{1,0},{2,1},{3,2},{4,7},{5,4},{6,5},{7,6},{8,11},{9,8},{10,9... | collective-permute-start | bytes 1572872 | tf_op jit(solution)/shard_map/ppermute | solution.py:67
  3.5 24.4 %collective-permute-start.1 = (bf16[1024,256]{1,0:T(8,128)(2,1)}, bf16[1024,256]{1,0:T(8,128)(2,1)}, u32[]{:S(2)}, u32[]{:S(2)}) collective-permute-start(bf16[1024,256]{1,0:T(8,128)(2,1)} %param.11), channel_id=1, source_target_pairs={{0,2},{1,3},{2,0},{3,1},{4,6},{5,7},{6,4},{7,5},{8,10},{9,11},{10,... | collective-permute-start | bytes 1572872 | tf_op jit(solution)/shard_map/ppermute | solution.py:67
  15.2 16.4 %copy-start.2 = (bf16[1024,3,256]{0,2,1:T(8,128)(2,1)}, bf16[1024,3,256]{0,2,1:T(8,128)(2,1)S(1)}, u32[]{:S(2)}) copy-start(bf16[1024,3,256]{0,2,1:T(8,128)(2,1)S(1)} %copy.67) | copy-start | bytes 4718596
  33.7 12.6 %copy-start.25 = (pred[1024]{0:T(1024)(128)(4,1)S(1)}, pred[1024]{0:T(1024)(128)(4,1)}, u32[]{:S(2)}) copy-start(pred[1024]{0:T(1024)(128)(4,1)} %get-tuple-element.49) | copy-start | bytes 3076
  35.7 10.6 %collective-permute-start.3 = (bf16[3,768]{0,1:T(8,128)(2,1)S(1)}, bf16[3,768]{0,1:T(8,128)(2,1)S(1)}, u32[]{:S(2)}, u32[]{:S(2)}) collective-permute-start(bf16[3,768]{0,1:T(8,128)(2,1)S(1)} %slice.169), channel_id=1, source_target_pairs={{0,4},{4,8},{8,12},{12,16},{16,20},{20,24},{24,28},{28,32},{32,36}... | collective-permute-start | bytes 13832 | tf_op jit(solution)/shard_map/ppermute | solution.py:19
  55.3 16.7 %copy-start.14 = (s32[1040]{0:T(1024)S(1)}, s32[1040]{0:T(1024)}, u32[]{:S(2)}) copy-start(s32[1040]{0:T(1024)} %iota_add_fusion) | copy-start | bytes 12484
  55.3 16.7 %copy-start.21 = (pred[1040]{0:T(1024)(128)(4,1)S(1)}, pred[1040]{0:T(1024)(128)(4,1)}, u32[]{:S(2)}) copy-start(pred[1040]{0:T(1024)(128)(4,1)} %get-tuple-element.51) | copy-start | bytes 3124
  55.3 16.7 %copy-start.22 = (pred[1040]{0:T(1024)(128)(4,1)S(1)}, pred[1040]{0:T(1024)(128)(4,1)}, u32[]{:S(2)}) copy-start(pred[1040]{0:T(1024)(128)(4,1)} %get-tuple-element.52) | copy-start | bytes 3124
  55.4 12.6 %collective-permute-start.4 = (bf16[2,256,512]{1,2,0:T(8,128)(2,1)S(1)}, bf16[2,256,512]{1,2,0:T(8,128)(2,1)S(1)}, u32[]{:S(2)}, u32[]{:S(2)}) collective-permute-start(bf16[2,256,512]{1,2,0:T(8,128)(2,1)S(1)} %pad_maximum_fusion.3), channel_id=1, source_target_pairs={{0,4},{4,8},{8,12},{12,16},{16,20},{20,24},{24,28},{28,32},{32,36}... | collective-permute-start | bytes 1572872 | tf_op jit(solution)/shard_map/ppermute | solution.py:19
  69.8 14.0 %collective-permute-start.5 = (bf16[2,256,512]{1,2,0:T(8,128)(2,1)}, bf16[2,256,512]{1,2,0:T(8,128)(2,1)}, u32[]{:S(2)}, u32[]{:S(2)}) collective-permute-start(bf16[2,256,512]{1,2,0:T(8,128)(2,1)} %pad_maximum_fusion.4), channel_id=1, source_target_pairs={{0,8},{4,12},{8,16},{12,20},{16,24},{20,28},{24,32},{28,36},{32,40... | collective-permute-start | bytes 1572872 | tf_op jit(solution)/shard_map/ppermute | solution.py:19
  86.7 25.0 %collective-permute-start.6 = (bf16[2,256,512]{1,2,0:T(8,128)(2,1)S(1)}, bf16[2,256,512]{1,2,0:T(8,128)(2,1)S(1)}, u32[]{:S(2)}, u32[]{:S(2)}) collective-permute-start(bf16[2,256,512]{1,2,0:T(8,128)(2,1)S(1)} %pad_maximum_fusion.5), channel_id=1, source_target_pairs={{0,16},{4,20},{8,24},{12,28},{16,32},{20,36},{24,40},{28,44},{32,4... | collective-permute-start | bytes 1572872 | tf_op jit(solution)/shard_map/ppermute | solution.py:19
  89.0 25.7 %copy-start.7 = (pred[512,1040]{0,1:T(8,128)(4,1)S(1)}, pred[512,1040]{0,1:T(8,128)(4,1)}, u32[]{:S(2)}) copy-start(pred[512,1040]{0,1:T(8,128)(4,1)} %get-tuple-element.30) | copy-start | bytes 1597444
  89.0 25.7 %copy-start.9 = (bf16[1024,2,128]{2,0,1:T(8,128)(2,1)S(1)}, bf16[1024,2,128]{2,0,1:T(8,128)(2,1)}, u32[]{:S(2)}) copy-start(bf16[1024,2,128]{2,0,1:T(8,128)(2,1)} %copy-done.8) | copy-start | bytes 1572868
  112.7 21.2 %collective-permute-start.7 = (bf16[2,256,512]{1,2,0:T(8,128)(2,1)S(1)}, bf16[2,256,512]{1,2,0:T(8,128)(2,1)S(1)}, u32[]{:S(2)}, u32[]{:S(2)}) collective-permute-start(bf16[2,256,512]{1,2,0:T(8,128)(2,1)S(1)} %pad_maximum_fusion.6), channel_id=1, source_target_pairs={{0,32},{4,36},{8,40},{12,44},{16,48},{20,52},{24,56},{28,60},{32,6... | collective-permute-start | bytes 1572872 | tf_op jit(solution)/shard_map/ppermute | solution.py:19
  120.6 30.3 %copy-start.11 = (bf16[1024,1,2,128]{3,0,2,1:T(8,128)(2,1)S(1)}, bf16[1024,1,2,128]{3,0,2,1:T(8,128)(2,1)}, u32[]{:S(2)}) copy-start(bf16[1024,1,2,128]{3,0,2,1:T(8,128)(2,1)} %copy.104) | copy-start | bytes 1572868
  120.6 30.3 %copy-start.23 = (bf16[16,2,128]{2,0,1:T(8,128)(2,1)S(1)}, bf16[16,2,128]{2,0,1:T(8,128)(2,1)}, u32[]{:S(2)}) copy-start(bf16[16,2,128]{2,0,1:T(8,128)(2,1)} %copy.69) | copy-start | bytes 24580
  135.6 24.1 %collective-permute-start.8 = (bf16[2,128,512]{1,2,0:T(8,128)(2,1)}, bf16[2,128,512]{1,2,0:T(8,128)(2,1)}, u32[]{:S(2)}, u32[]{:S(2)}) collective-permute-start(bf16[2,128,512]{1,2,0:T(8,128)(2,1)} %pad_maximum_fusion.13), channel_id=1, source_target_pairs={{0,4},{4,8},{8,12},{12,16},{16,20},{20,24},{24,28},{28,32},{32,36}... | collective-permute-start | bytes 786440 | tf_op jit(solution)/shard_map/ppermute | solution.py:19
  138.2 21.4 %collective-permute-start.9 = (bf16[2,256,256]{1,2,0:T(8,128)(2,1)}, bf16[2,256,256]{1,2,0:T(8,128)(2,1)}, u32[]{:S(2)}, u32[]{:S(2)}) collective-permute-start(bf16[2,256,256]{1,2,0:T(8,128)(2,1)} %pad_maximum_fusion.14), channel_id=1, source_target_pairs={{0,68},{4,72},{8,76},{12,80},{16,84},{20,88},{24,92},{28,96},{32,1... | collective-permute-start | bytes 786440 | tf_op jit(solution)/shard_map/ppermute | solution.py:19
  161.7 49.6 %copy-start.4 = (bf16[1024,256]{1,0:T(8,128)(2,1)S(1)}, bf16[1024,256]{1,0:T(8,128)(2,1)}, u32[]{:S(2)}) copy-start(bf16[1024,256]{1,0:T(8,128)(2,1)} %param.11) | copy-start | bytes 1572868
  162.3 56.2 %copy-start.5 = (bf16[1024,704]{0,1:T(8,128)(2,1)S(1)}, bf16[1024,704]{0,1:T(8,128)(2,1)}, u32[]{:S(2)}) copy-start(bf16[1024,704]{0,1:T(8,128)(2,1)} %param.20) | copy-start | bytes 4325380
  163.1 30.5 %collective-permute-start.10 = (bf16[1024,256]{1,0:T(8,128)(2,1)S(1)}, bf16[1024,256]{1,0:T(8,128)(2,1)S(1)}, u32[]{:S(2)}, u32[]{:S(2)}) collective-permute-start(bf16[1024,256]{1,0:T(8,128)(2,1)S(1)} %convolution_convert_fusion.3), channel_id=1, source_target_pairs={{0,1},{1,2},{2,3},{3,0},{4,5},{5,6},{6,7},{7,4},{8,9},{9,10},{10,1... | collective-permute-start | bytes 1572872 | tf_op jit(solution)/shard_map/ppermute | solution.py:92
  165.6 36.7 %collective-permute-start.11 = (bf16[1024,256]{1,0:T(8,128)(2,1)S(1)}, bf16[1024,256]{1,0:T(8,128)(2,1)S(1)}, u32[]{:S(2)}, u32[]{:S(2)}) collective-permute-start(bf16[1024,256]{1,0:T(8,128)(2,1)S(1)} %convolution_convert_fusion.2), channel_id=1, source_target_pairs={{0,2},{1,3},{2,0},{3,1},{4,6},{5,7},{6,4},{7,5},{8,10},{9,11},{10,... | collective-permute-start | bytes 1572872 | tf_op jit(solution)/shard_map/ppermute | solution.py:92
  189.6 21.7 %collective-permute-start.12 = (bf16[1024,256]{1,0:T(8,128)(2,1)S(1)}, bf16[1024,256]{1,0:T(8,128)(2,1)S(1)}, u32[]{:S(2)}, u32[]{:S(2)}) collective-permute-start(bf16[1024,256]{1,0:T(8,128)(2,1)S(1)} %convolution_convert_fusion.1), channel_id=1, source_target_pairs={{0,3},{1,0},{2,1},{3,2},{4,7},{5,4},{6,5},{7,6},{8,11},{9,8},{10,9... | collective-permute-start | bytes 1572872 | tf_op jit(solution)/shard_map/ppermute | solution.py:92
  211.9 17.0 %collective-permute-start.15 = (bf16[1024,256]{1,0:T(8,128)(2,1)S(1)}, bf16[1024,256]{1,0:T(8,128)(2,1)S(1)}, u32[]{:S(2)}, u32[]{:S(2)}) collective-permute-start(bf16[1024,256]{1,0:T(8,128)(2,1)S(1)} %get-tuple-element.46), channel_id=1, source_target_pairs={{0,3},{1,0},{2,1},{3,2},{4,7},{5,4},{6,5},{7,6},{8,11},{9,8},{10,9... | collective-permute-start | bytes 1572872 | tf_op jit(solution)/shard_map/ppermute | solution.py:67
  216.5 22.7 %collective-permute-start.14 = (bf16[1024,256]{1,0:T(8,128)(2,1)S(1)}, bf16[1024,256]{1,0:T(8,128)(2,1)S(1)}, u32[]{:S(2)}, u32[]{:S(2)}) collective-permute-start(bf16[1024,256]{1,0:T(8,128)(2,1)S(1)} %get-tuple-element.46), channel_id=1, source_target_pairs={{0,2},{1,3},{2,0},{3,1},{4,6},{5,7},{6,4},{7,5},{8,10},{9,11},{10,... | collective-permute-start | bytes 1572872 | tf_op jit(solution)/shard_map/ppermute | solution.py:67
  216.5 24.5 %collective-permute-start.13 = (bf16[1024,256]{1,0:T(8,128)(2,1)S(1)}, bf16[1024,256]{1,0:T(8,128)(2,1)S(1)}, u32[]{:S(2)}, u32[]{:S(2)}) collective-permute-start(bf16[1024,256]{1,0:T(8,128)(2,1)S(1)} %get-tuple-element.46), channel_id=1, source_target_pairs={{0,1},{1,2},{2,3},{3,0},{4,5},{5,6},{6,7},{7,4},{8,9},{9,10},{10,1... | collective-permute-start | bytes 1572872 | tf_op jit(solution)/shard_map/ppermute | solution.py:67
  247.8 16.4 %collective-permute-start.16 = (bf16[1024,256]{1,0:T(8,128)(2,1)S(1)}, bf16[1024,256]{1,0:T(8,128)(2,1)S(1)}, u32[]{:S(2)}, u32[]{:S(2)}) collective-permute-start(bf16[1024,256]{1,0:T(8,128)(2,1)S(1)} %convolution_convert_fusion.7), channel_id=1, source_target_pairs={{0,1},{1,2},{2,3},{3,0},{4,5},{5,6},{6,7},{7,4},{8,9},{9,10},{10,1... | collective-permute-start | bytes 1572872 | tf_op jit(solution)/shard_map/ppermute | solution.py:92
  248.7 15.5 %collective-permute-start.17 = (bf16[1024,256]{1,0:T(8,128)(2,1)S(1)}, bf16[1024,256]{1,0:T(8,128)(2,1)S(1)}, u32[]{:S(2)}, u32[]{:S(2)}) collective-permute-start(bf16[1024,256]{1,0:T(8,128)(2,1)S(1)} %convolution_convert_fusion.6), channel_id=1, source_target_pairs={{0,2},{1,3},{2,0},{3,1},{4,6},{5,7},{6,4},{7,5},{8,10},{9,11},{10,... | collective-permute-start | bytes 1572872 | tf_op jit(solution)/shard_map/ppermute | solution.py:92
  249.1 24.5 %collective-permute-start.18 = (bf16[1024,256]{1,0:T(8,128)(2,1)S(1)}, bf16[1024,256]{1,0:T(8,128)(2,1)S(1)}, u32[]{:S(2)}, u32[]{:S(2)}) collective-permute-start(bf16[1024,256]{1,0:T(8,128)(2,1)S(1)} %convolution_convert_fusion.5), channel_id=1, source_target_pairs={{0,3},{1,0},{2,1},{3,2},{4,7},{5,4},{6,5},{7,6},{8,11},{9,8},{10,9... | collective-permute-start | bytes 1572872 | tf_op jit(solution)/shard_map/ppermute | solution.py:92
  (20 other events, 75.4 us)
where the time goes:
time: 278 us; the launch traced here: 275 us
  waiting for transfers between devices  125 us (45%)
  starting transfers between devices  71.2 us (26%)
  matrix products  43.2 us (16%)
  other arithmetic  24.8 us (9%)
  local copies, waits for them, and re-layouts  9.15 us (3%)
    ppermute x7, waiting for transfers between devices, passed_along(): return lax.ppermute(block, axis, route)  61.2 us
    ppermute x6, waiting for transfers between devices, scattered_sum(): lax.ppermute(block((index + distance) % count), axis, group_route(axis, d...  38.2 us
    ppermute x6, starting transfers between devices, scattered_sum(): lax.ppermute(block((index + distance) % count), axis, group_route(axis, d...  35.9 us
    ppermute x6, waiting for transfers between devices, gathered_products(): arrived = lax.ppermute(local, axis, group_route(axis, distance))  25.3 us
    ppermute x7, starting transfers between devices, passed_along(): return lax.ppermute(block, axis, route)  24.4 us
    dot_general x12, matrix products, gathered_products(): term = jnp.dot(piece, rows, preferred_element_type=jnp.float32)  13.3 us
    ppermute x6, starting transfers between devices, gathered_products(): arrived = lax.ppermute(local, axis, group_route(axis, distance))  10.9 us
    dot_general x2, matrix products, body(): jnp.einsum('hqk,khd->qhd', probs, values_all, preferred_element_type=jnp....  8.7 us
  transfers between devices with their start and end apart: 19, of which 14 were waited for; matrix products, arithmetic and copies ran while one was open for 15% of the time, Pallas kernels for 0%

commit v1 on v0

--- a/solution.py
+++ b/solution.py
@@ -54,18 +54,31 @@
     return exact_product(near_map, earlier) + from_pair(last[..., width:])
 
 
-def group_route(axis, distance):
+def ring_place(index):
+    return (index % 2) * 2 + index // 2
+
+
+def ring_route(axis, step):
     count = lax.axis_size(axis)
-    return [(i, (i + distance) % count) for i in range(count)]
+    return [(i, ring_place((ring_place(i) + step) % count)) for i in range(count)]
 
 
 def gathered_products(local, weights, axis):
     count, index = (lax.axis_size(axis), lax.axis_index(axis))
     width = local.shape[1]
-    pieces = [(local, index)]
-    for distance in range(1, count):
-        arrived = lax.ppermute(local, axis, group_route(axis, distance))
-        pieces.append((arrived, (index - distance) % count))
+    place = ring_place(index)
+    half = local.shape[0] // 2
+    from_left = lax.ppermute(local, axis, ring_route(axis, 1))
+    from_right = lax.ppermute(local, axis, ring_route(axis, -1))
+    far_top = lax.ppermute(from_left[:half], axis, ring_route(axis, 1))
+    far_bottom = lax.ppermute(from_right[half:], axis, ring_route(axis, -1))
+    far = jnp.concatenate([far_top, far_bottom], 0)
+    pieces = [
+        (local, index),
+        (from_left, ring_place((place - 1) % count)),
+        (from_right, ring_place((place + 1) % count)),
+        (far, ring_place((place + 2) % count)),
+    ]
     totals = [None] * len(weights)
     squares = None
     for piece, source in pieces:
@@ -82,17 +95,32 @@
 def scattered_sum(left, weight, axis):
     count, index = (lax.axis_size(axis), lax.axis_index(axis))
     width = weight.shape[1] // count
-
-    def block(owner):
+    place = ring_place(index)
+    half = left.shape[0] // 2
+
+    def block(owner_place, rows=slice(None)):
+        owner = ring_place(owner_place % count)
         cols = lax.dynamic_slice_in_dim(weight, owner * width, width, 1)
-        return jnp.dot(left, cols, preferred_element_type=jnp.float32).astype(jnp.bfloat16)
-
-    total = None
-    for distance in range(1, count):
-        arrived = lax.ppermute(block((index + distance) % count), axis, group_route(axis, distance))
-        total = arrived.astype(jnp.float32) if total is None else total + arrived.astype(jnp.float32)
-    own = block(index).astype(jnp.float32)
-    return own if total is None else total + own
+        return jnp.dot(left[rows], cols, preferred_element_type=jnp.float32)
+
+    relay_top = lax.ppermute(
+        block(place + 2, slice(0, half)).astype(jnp.bfloat16), axis, ring_route(axis, 1)
+    )
+    relay_bottom = lax.ppermute(
+        block(place + 2, slice(half, None)).astype(jnp.bfloat16), axis, ring_route(axis, -1)
+    )
+    right_block = block(place + 1).astype(jnp.bfloat16).astype(jnp.float32)
+    right_block = jnp.concatenate(
+        [right_block[:half] + relay_top.astype(jnp.float32), right_block[half:]], 0
+    )
+    left_block = block(place - 1).astype(jnp.bfloat16).astype(jnp.float32)
+    left_block = jnp.concatenate(
+        [left_block[:half], left_block[half:] + relay_bottom.astype(jnp.float32)], 0
+    )
+    from_left = lax.ppermute(right_block.astype(jnp.bfloat16), axis, ring_route(axis, 1))
+    from_right = lax.ppermute(left_block.astype(jnp.bfloat16), axis, ring_route(axis, -1))
+    own = block(place).astype(jnp.bfloat16).astype(jnp.float32)
+    return own + from_left.astype(jnp.float32) + from_right.astype(jnp.float32)
 
 
 def unit_rows(values_in):

time: 278 us -> 287 us (1.032)
  waiting for transfers between devices: 125 us -> 89.2 us
  starting transfers between devices: 71.2 us -> 96 us
  local copies, waits for them, and re-layouts: 9.15 us -> 22.7 us
  other arithmetic: 24.8 us -> 29 us
    ppermute x7, starting transfers between devices: 24.4 us -> 59.9 us  [passed_along(): return lax.ppermute(block, axis, route)]
    ppermute x12 -> x16, waiting for transfers between devices: 63.5 us -> 42 us  [the longest x2 14.2 us: scattered_sum(): lax.ppermute(right_block.astype(jnp.bfloat16), axis, ring_route(axis, 1))]
    ppermute x7, waiting for transfers between devices: 61.2 us -> 47.2 us  [passed_along(): return lax.ppermute(block, axis, route)]
    ppermute x12 -> x16, starting transfers between devices: 46.8 us -> 36.1 us  [the longest x2 16.3 us: scattered_sum(): lax.ppermute(right_block.astype(jnp.bfloat16), axis, ring_route(axis, 1))]
    mul x4, local copies, waits for them, and re-layouts: 0.03 us -> 5.09 us  [body(): taps[offset] * shifted]
    unnamed x70 -> x55, local copies, waits for them, and re-layouts: 5.03 us -> 6.66 us
    reduce_sum x7 -> x8, other arithmetic: 6.26 us -> 5.39 us  [gathered_products(): part_sq = jnp.sum(piece_f * piece_f, -1)]
  transfers between devices with their start and end apart: 19 -> 23, of which waited for: 14 -> 13; matrix products, arithmetic and copies ran while one was open for 15% -> 22% of each run, Pallas kernels for 0% -> 0%
where the time goes in v1:
time: 287 us; the launch traced here: 282 us
  starting transfers between devices  96 us (33%)
  waiting for transfers between devices  89.2 us (31%)
  matrix products  42.2 us (15%)
  other arithmetic  29 us (10%)
  local copies, waits for them, and re-layouts  22.7 us (8%)
    ppermute x7, starting transfers between devices, passed_along(): return lax.ppermute(block, axis, route)  59.9 us
    ppermute x7, waiting for transfers between devices, passed_along(): return lax.ppermute(block, axis, route)  47.2 us
    ppermute x2, starting transfers between devices, scattered_sum(): lax.ppermute(right_block.astype(jnp.bfloat16), axis, ring_route(axis, 1))  16.3 us
    ppermute x2, waiting for transfers between devices, scattered_sum(): lax.ppermute(right_block.astype(jnp.bfloat16), axis, ring_route(axis, 1))  14.2 us
    dot_general x12, matrix products, gathered_products(): term = jnp.dot(piece, rows, preferred_element_type=jnp.float32)  12 us
    ppermute x2, waiting for transfers between devices, scattered_sum(): lax.ppermute(block(place + 2, slice(0, half)).astype(jnp.bfloat16), axis,...  9.56 us
    dot_general x2, matrix products, body(): jnp.einsum('hqk,khd->qhd', probs, values_all, preferred_element_type=jnp....  9.5 us
    ppermute x2, waiting for transfers between devices, scattered_sum(): lax.ppermute(left_block.astype(jnp.bfloat16), axis, ring_route(axis, -1))  8.59 us
  transfers between devices with their start and end apart: 23, of which 13 were waited for; matrix products, arithmetic and copies ran while one was open for 22% of the time, Pallas kernels for 0%

profile of v1, /device:TPU:14, one launch (start us, length us, event | category | flops | bytes accessed | tf_op | source)
XLA Modules:
  0.0 281.7 jit_solution(17410152266242385348)
XLA Ops:
  0.8 2.4 collective-permute-start
  22.8 3.3 %collective-permute-start.2 = (bf16[512,256]{1,0:T(8,128)(2,1)S(1)}, bf16[512,256]{1,0:T(8,128)(2,1)S(1)}, u32[]{:S(2)}, u32[]{:S(2)}) collective-permute-start(bf16[512,256]{1,0:T(8,128)(2,1)S(1)} %slice.261), channel_id=1, source_target_pairs={{0,2},{1,3},{2,1},{3,0},{4,6},{5,7},{6,5},{7,4},{8,10},{9,11},{10,... | collective-permute-start | bytes 786440 | tf_op jit(solution)/shard_map/ppermute | solution.py:73
  34.7 1.9 collective-permute-start.4
  46.2 4.2 %select_add_fusion = f32[1024,768]{0,1:T(8,128)S(1)} fusion(bf16[1024,768]{0,1:T(8,128)(2,1)S(1)} %fusion.5, bf16[3,768]{0,1:T(8,128)(2,1)} %collective-permute-done.4, f32[768]{0:T(1024)} %mul.347, f32[768]{0:T(1024)} %mul.344, f32[768]{0:T(1024)} %mul.341, f32[768]{0:T(1024)} %mul.323, pred[1024]{0:T(1024)(128)(4,1)} %get-tuple-element.52, ...), kind=kLoop, calls=%fused_computation.11 | loop fusion | flops 18874368 | bytes 4739584 | tf_op jit(solution)/shard_map/add | solution.py:167
  56.9 3.9 %collective-permute-start.5 = (bf16[2,256,512]{1,2,0:T(8,128)(2,1)S(1)}, bf16[2,256,512]{1,2,0:T(8,128)(2,1)S(1)}, u32[]{:S(2)}, u32[]{:S(2)}) collective-permute-start(bf16[2,256,512]{1,2,0:T(8,128)(2,1)S(1)} %pad_maximum_fusion.3), channel_id=1, source_target_pairs={{0,4},{4,8},{8,12},{12,16},{16,20},{20,24},{24,28},{28,32},{32,36}... | collective-permute-start | bytes 1572872 | tf_op jit(solution)/shard_map/ppermute | solution.py:19
  61.6 8.2 %collective-permute-done.5 = bf16[2,256,512]{1,2,0:T(8,128)(2,1)S(1)} collective-permute-done((bf16[2,256,512]{1,2,0:T(8,128)(2,1)S(1)}, bf16[2,256,512]{1,2,0:T(8,128)(2,1)S(1)}, u32[]{:S(2)}, u32[]{:S(2)}) %collective-permute-start.5) | collective-permute-done | bytes 524320 | tf_op jit(solution)/shard_map/ppermute | solution.py:19
  72.3 2.2 collective-permute-start.6
  74.5 2.0 fusion.9
  78.1 9.6 %collective-permute-done.6 = bf16[2,256,512]{1,2,0:T(8,128)(2,1)} collective-permute-done((bf16[2,256,512]{1,2,0:T(8,128)(2,1)}, bf16[2,256,512]{1,2,0:T(8,128)(2,1)}, u32[]{:S(2)}, u32[]{:S(2)}) %collective-permute-start.6) | collective-permute-done | bytes 524320 | tf_op jit(solution)/shard_map/ppermute | solution.py:19
  90.7 3.7 %collective-permute-start.7 = (bf16[2,256,512]{1,2,0:T(8,128)(2,1)S(1)}, bf16[2,256,512]{1,2,0:T(8,128)(2,1)S(1)}, u32[]{:S(2)}, u32[]{:S(2)}) collective-permute-start(bf16[2,256,512]{1,2,0:T(8,128)(2,1)S(1)} %pad_maximum_fusion.5), channel_id=1, source_target_pairs={{0,16},{4,20},{8,24},{12,28},{16,32},{20,36},{24,40},{28,44},{32,4... | collective-permute-start | bytes 1572872 | tf_op jit(solution)/shard_map/ppermute | solution.py:19
  95.2 21.4 %collective-permute-done.7 = bf16[2,256,512]{1,2,0:T(8,128)(2,1)S(1)} collective-permute-done((bf16[2,256,512]{1,2,0:T(8,128)(2,1)S(1)}, bf16[2,256,512]{1,2,0:T(8,128)(2,1)S(1)}, u32[]{:S(2)}, u32[]{:S(2)}) %collective-permute-start.7) | collective-permute-done | bytes 524320 | tf_op jit(solution)/shard_map/ppermute | solution.py:19
  117.5 1.9 collective-permute-start.8
  119.5 3.0 %fusion.3 = f32[2,512,1040]{1,2,0:T(8,128)} fusion(pred[512,1040]{0,1:T(8,128)(4,1)S(1)} %copy-done.5, bf16[1024,2,128]{2,0,1:T(8,128)(2,1)S(1)} %copy-done.7, bf16[16,2,128]{2,0,1:T(8,128)(2,1)S(1)} %copy-done.17, bf16[1024,2,128]{2,0,1:T(8,128)(2,1)S(1)} %fusion.28), kind=kOutput, calls=%fused_computation.5 | convolution fusion | flops 275824640 | bytes 5586944 | tf_op jit(solution)/shard_map/qhd,khd->hqk/dot_general | solution.py:210
  122.4 3.0 %fusion.1 = f32[2,512,1040]{1,2,0:T(8,128)} fusion(pred[512,1040]{0,1:T(8,128)(4,1)S(1)} %copy-done.4, bf16[1024,2,128]{2,0,1:T(8,128)(2,1)S(1)} %copy-done.7, bf16[16,2,128]{2,0,1:T(8,128)(2,1)S(1)} %copy-done.17, bf16[1024,2,128]{2,0,1:T(8,128)(2,1)S(1)} %fusion.28), kind=kOutput, calls=%fused_computation.3 | convolution fusion | flops 275824640 | bytes 5586944 | tf_op jit(solution)/shard_map/qhd,khd->hqk/dot_general | solution.py:210
  125.5 8.0 %collective-permute-done.8 = bf16[2,256,512]{1,2,0:T(8,128)(2,1)S(1)} collective-permute-done((bf16[2,256,512]{1,2,0:T(8,128)(2,1)S(1)}, bf16[2,256,512]{1,2,0:T(8,128)(2,1)S(1)}, u32[]{:S(2)}, u32[]{:S(2)}) %collective-permute-start.8) | collective-permute-done | bytes 524320 | tf_op jit(solution)/shard_map/ppermute | solution.py:19
  135.2 1.9 collective-permute-start.9
  137.8 44.3 %collective-permute-start.10 = (bf16[2,256,256]{1,2,0:T(8,128)(2,1)}, bf16[2,256,256]{1,2,0:T(8,128)(2,1)}, u32[]{:S(2)}, u32[]{:S(2)}) collective-permute-start(bf16[2,256,256]{1,2,0:T(8,128)(2,1)} %pad_maximum_fusion.18), channel_id=1, source_target_pairs={{0,68},{4,72},{8,76},{12,80},{16,84},{20,88},{24,92},{28,96},{32,1... | collective-permute-start | bytes 786440 | tf_op jit(solution)/shard_map/ppermute | solution.py:19
  182.2 4.3 %fusion.16 = f32[512,2,128]{0,2,1:T(8,128)S(1)} fusion(f32[2,512,1040]{1,2,0:T(8,128)} %fusion.3, bf16[1024,2,128]{2,0,1:T(8,128)(2,1)S(1)} %bitcast.111, bf16[16,2,128]{2,0,1:T(8,128)(2,1)S(1)} %copy-done.18), kind=kOutput, calls=%fused_computation.41 | convolution fusion | flops 275826688 | bytes 5316608 | tf_op jit(solution)/shard_map/hqk,khd->qhd/dot_general | solution.py:218
  186.5 5.2 %fusion.17 = f32[512,2,128]{0,2,1:T(8,128)} fusion(f32[2,512,1040]{1,2,0:T(8,128)} %fusion.1, bf16[1024,2,128]{2,0,1:T(8,128)(2,1)S(1)} %bitcast.112, bf16[16,2,128]{2,0,1:T(8,128)(2,1)S(1)} %copy-done.18), kind=kOutput, calls=%fused_computation.42 | convolution fusion | flops 275826688 | bytes 5316608 | tf_op jit(solution)/shard_map/hqk,khd->qhd/dot_general | solution.py:218
  195.7 2.7 collective-permute-start.11
  199.1 4.1 %collective-permute-done.11 = bf16[512,256]{0,1:T(8,128)(2,1)S(1)} collective-permute-done((bf16[512,256]{0,1:T(8,128)(2,1)S(1)}, bf16[512,256]{0,1:T(8,128)(2,1)S(1)}, u32[]{:S(2)}, u32[]{:S(2)}) %collective-permute-start.11) | collective-permute-done | bytes 262176 | tf_op jit(solution)/shard_map/ppermute | solution.py:106
  203.4 12.6 %collective-permute-start.12 = (bf16[1024,256]{0,1:T(8,128)(2,1)S(1)}, bf16[1024,256]{0,1:T(8,128)(2,1)}, u32[]{:S(2)}, u32[]{:S(2)}) collective-permute-start(bf16[1024,256]{0,1:T(8,128)(2,1)S(1)} %pad_maximum_fusion.7), channel_id=1, source_target_pairs={{0,2},{1,3},{2,1},{3,0},{4,6},{5,7},{6,5},{7,4},{8,10},{9,11},{10,... | collective-permute-start | bytes 1572872 | tf_op jit(solution)/shard_map/ppermute | solution.py:120
  217.3 8.4 %collective-permute-done.12 = bf16[1024,256]{0,1:T(8,128)(2,1)} collective-permute-done((bf16[1024,256]{0,1:T(8,128)(2,1)S(1)}, bf16[1024,256]{0,1:T(8,128)(2,1)}, u32[]{:S(2)}, u32[]{:S(2)}) %collective-permute-start.12) | collective-permute-done | bytes 524320 | tf_op jit(solution)/shard_map/ppermute | solution.py:120
  225.7 4.7 %collective-permute-done.14 = bf16[1024,256]{0,1:T(8,128)(2,1)} collective-permute-done((bf16[1024,256]{0,1:T(8,128)(2,1)}, bf16[1024,256]{0,1:T(8,128)(2,1)}, u32[]{:S(2)}, u32[]{:S(2)}) %collective-permute-start.14) | collective-permute-done | bytes 524320 | tf_op jit(solution)/shard_map/ppermute | solution.py:121
  232.0 3.2 %collective-permute-start.15 = (bf16[1024,256]{0,1:T(8,128)(2,1)S(1)}, bf16[1024,256]{0,1:T(8,128)(2,1)S(1)}, u32[]{:S(2)}, u32[]{:S(2)}) collective-permute-start(bf16[1024,256]{0,1:T(8,128)(2,1)S(1)} %get-tuple-element.10), channel_id=1, source_target_pairs={{0,2},{1,3},{2,1},{3,0},{4,6},{5,7},{6,5},{7,4},{8,10},{9,11},{10,... | collective-permute-start | bytes 1572872 | tf_op jit(solution)/shard_map/ppermute | solution.py:71
  236.4 7.9 %collective-permute-done.16 = bf16[1024,256]{0,1:T(8,128)(2,1)S(1)} collective-permute-done((bf16[1024,256]{0,1:T(8,128)(2,1)S(1)}, bf16[1024,256]{0,1:T(8,128)(2,1)S(1)}, u32[]{:S(2)}, u32[]{:S(2)}) %collective-permute-start.16) | collective-permute-done | bytes 524320 | tf_op jit(solution)/shard_map/ppermute | solution.py:72
  244.4 3.3 %collective-permute-start.17 = (bf16[512,256]{0,1:T(8,128)(2,1)S(1)}, bf16[512,256]{0,1:T(8,128)(2,1)S(1)}, u32[]{:S(2)}, u32[]{:S(2)}) collective-permute-start(bf16[512,256]{0,1:T(8,128)(2,1)S(1)} %slice.298), channel_id=1, source_target_pairs={{0,2},{1,3},{2,1},{3,0},{4,6},{5,7},{6,5},{7,4},{8,10},{9,11},{10,... | collective-permute-start | bytes 786440 | tf_op jit(solution)/shard_map/ppermute | solution.py:73
  255.8 3.6 %collective-permute-start.19 = (bf16[512,256]{0,1:T(8,128)(2,1)S(1)}, bf16[512,256]{0,1:T(8,128)(2,1)S(1)}, u32[]{:S(2)}, u32[]{:S(2)}) collective-permute-start(bf16[512,256]{0,1:T(8,128)(2,1)S(1)} %convolution_convert_fusion.9), channel_id=1, source_target_pairs={{0,2},{1,3},{2,1},{3,0},{4,6},{5,7},{6,5},{7,4},{8,10},{9,11},{10,... | collective-permute-start | bytes 786440 | tf_op jit(solution)/shard_map/ppermute | solution.py:106
  260.1 5.4 %collective-permute-done.19 = bf16[512,256]{0,1:T(8,128)(2,1)S(1)} collective-permute-done((bf16[512,256]{0,1:T(8,128)(2,1)S(1)}, bf16[512,256]{0,1:T(8,128)(2,1)S(1)}, u32[]{:S(2)}, u32[]{:S(2)}) %collective-permute-start.19) | collective-permute-done | bytes 262176 | tf_op jit(solution)/shard_map/ppermute | solution.py:106
  265.7 3.8 %collective-permute-start.20 = (bf16[1024,256]{0,1:T(8,128)(2,1)S(1)}, bf16[1024,256]{0,1:T(8,128)(2,1)S(1)}, u32[]{:S(2)}, u32[]{:S(2)}) collective-permute-start(bf16[1024,256]{0,1:T(8,128)(2,1)S(1)} %pad_maximum_fusion.9), channel_id=1, source_target_pairs={{0,2},{1,3},{2,1},{3,0},{4,6},{5,7},{6,5},{7,4},{8,10},{9,11},{10,... | collective-permute-start | bytes 1572872 | tf_op jit(solution)/shard_map/ppermute | solution.py:120
  270.4 5.8 %collective-permute-done.20 = bf16[1024,256]{0,1:T(8,128)(2,1)S(1)} collective-permute-done((bf16[1024,256]{0,1:T(8,128)(2,1)S(1)}, bf16[1024,256]{0,1:T(8,128)(2,1)S(1)}, u32[]{:S(2)}, u32[]{:S(2)}) %collective-permute-start.20) | collective-permute-done | bytes 524320 | tf_op jit(solution)/shard_map/ppermute | solution.py:120
  276.2 3.9 %collective-permute-done.22 = bf16[1024,256]{0,1:T(8,128)(2,1)S(1)} collective-permute-done((bf16[1024,256]{0,1:T(8,128)(2,1)S(1)}, bf16[1024,256]{0,1:T(8,128)(2,1)S(1)}, u32[]{:S(2)}, u32[]{:S(2)}) %collective-permute-start.22) | collective-permute-done | bytes 524320 | tf_op jit(solution)/shard_map/ppermute | solution.py:121
  (186 shorter events, 75.3 us)
Async XLA Ops:
  0.0 235.2 %copy-start = (bf16[1024,704]{0,1:T(8,128)(2,1)S(1)}, bf16[1024,704]{0,1:T(8,128)(2,1)}, u32[]{:S(2)}) copy-start(bf16[1024,704]{0,1:T(8,128)(2,1)} %param.19) | copy-start | bytes 4325380
  0.0 20.7 %collective-permute-start.1 = (bf16[1024,256]{1,0:T(8,128)(2,1)}, bf16[1024,256]{1,0:T(8,128)(2,1)}, u32[]{:S(2)}, u32[]{:S(2)}) collective-permute-start(bf16[1024,256]{1,0:T(8,128)(2,1)} %param.11), channel_id=1, source_target_pairs={{0,3},{1,2},{2,0},{3,1},{4,7},{5,6},{6,4},{7,5},{8,11},{9,10},{10,... | collective-permute-start | bytes 1572872 | tf_op jit(solution)/shard_map/ppermute | solution.py:72
  0.8 20.9 %collective-permute-start = (bf16[1024,256]{1,0:T(8,128)(2,1)}, bf16[1024,256]{1,0:T(8,128)(2,1)}, u32[]{:S(2)}, u32[]{:S(2)}) collective-permute-start(bf16[1024,256]{1,0:T(8,128)(2,1)} %param.11), channel_id=1, source_target_pairs={{0,2},{1,3},{2,1},{3,0},{4,6},{5,7},{6,5},{7,4},{8,10},{9,11},{10,... | collective-permute-start | bytes 1572872 | tf_op jit(solution)/shard_map/ppermute | solution.py:71
  21.7 10.2 %collective-permute-start.3 = (bf16[512,256]{1,0:T(8,128)(2,1)S(1)}, bf16[512,256]{1,0:T(8,128)(2,1)S(1)}, u32[]{:S(2)}, u32[]{:S(2)}) collective-permute-start(bf16[512,256]{1,0:T(8,128)(2,1)S(1)} %slice.262), channel_id=1, source_target_pairs={{0,3},{1,2},{2,0},{3,1},{4,7},{5,6},{6,4},{7,5},{8,11},{9,10},{10,... | collective-permute-start | bytes 786440 | tf_op jit(solution)/shard_map/ppermute | solution.py:74
  22.8 9.1 %collective-permute-start.2 = (bf16[512,256]{1,0:T(8,128)(2,1)S(1)}, bf16[512,256]{1,0:T(8,128)(2,1)S(1)}, u32[]{:S(2)}, u32[]{:S(2)}) collective-permute-start(bf16[512,256]{1,0:T(8,128)(2,1)S(1)} %slice.261), channel_id=1, source_target_pairs={{0,2},{1,3},{2,1},{3,0},{4,6},{5,7},{6,5},{7,4},{8,10},{9,11},{10,... | collective-permute-start | bytes 786440 | tf_op jit(solution)/shard_map/ppermute | solution.py:73
  34.7 11.5 %collective-permute-start.4 = (bf16[3,768]{0,1:T(8,128)(2,1)}, bf16[3,768]{0,1:T(8,128)(2,1)}, u32[]{:S(2)}, u32[]{:S(2)}) collective-permute-start(bf16[3,768]{0,1:T(8,128)(2,1)} %slice.263), channel_id=1, source_target_pairs={{0,4},{4,8},{8,12},{12,16},{16,20},{20,24},{24,28},{28,32},{32,36}... | collective-permute-start | bytes 13832 | tf_op jit(solution)/shard_map/ppermute | solution.py:19
  56.8 17.7 %copy-start.13 = (s32[1040]{0:T(1024)S(1)}, s32[1040]{0:T(1024)}, u32[]{:S(2)}) copy-start(s32[1040]{0:T(1024)} %iota_add_fusion) | copy-start | bytes 12484
  56.8 17.7 %copy-start.15 = (pred[1040]{0:T(1024)(128)(4,1)S(1)}, pred[1040]{0:T(1024)(128)(4,1)}, u32[]{:S(2)}) copy-start(pred[1040]{0:T(1024)(128)(4,1)} %get-tuple-element.53) | copy-start | bytes 3124
  56.9 12.8 %collective-permute-start.5 = (bf16[2,256,512]{1,2,0:T(8,128)(2,1)S(1)}, bf16[2,256,512]{1,2,0:T(8,128)(2,1)S(1)}, u32[]{:S(2)}, u32[]{:S(2)}) collective-permute-start(bf16[2,256,512]{1,2,0:T(8,128)(2,1)S(1)} %pad_maximum_fusion.3), channel_id=1, source_target_pairs={{0,4},{4,8},{8,12},{12,16},{16,20},{20,24},{24,28},{28,32},{32,36}... | collective-permute-start | bytes 1572872 | tf_op jit(solution)/shard_map/ppermute | solution.py:19
  72.3 15.3 %collective-permute-start.6 = (bf16[2,256,512]{1,2,0:T(8,128)(2,1)}, bf16[2,256,512]{1,2,0:T(8,128)(2,1)}, u32[]{:S(2)}, u32[]{:S(2)}) collective-permute-start(bf16[2,256,512]{1,2,0:T(8,128)(2,1)} %pad_maximum_fusion.4), channel_id=1, source_target_pairs={{0,8},{4,12},{8,16},{12,20},{16,24},{20,28},{24,32},{28,36},{32,40... | collective-permute-start | bytes 1572872 | tf_op jit(solution)/shard_map/ppermute | solution.py:19
  90.7 25.8 %collective-permute-start.7 = (bf16[2,256,512]{1,2,0:T(8,128)(2,1)S(1)}, bf16[2,256,512]{1,2,0:T(8,128)(2,1)S(1)}, u32[]{:S(2)}, u32[]{:S(2)}) collective-permute-start(bf16[2,256,512]{1,2,0:T(8,128)(2,1)S(1)} %pad_maximum_fusion.5), channel_id=1, source_target_pairs={{0,16},{4,20},{8,24},{12,28},{16,32},{20,36},{24,40},{28,44},{32,4... | collective-permute-start | bytes 1572872 | tf_op jit(solution)/shard_map/ppermute | solution.py:19
  94.8 24.7 %copy-start.5 = (pred[512,1040]{0,1:T(8,128)(4,1)S(1)}, pred[512,1040]{0,1:T(8,128)(4,1)}, u32[]{:S(2)}) copy-start(pred[512,1040]{0,1:T(8,128)(4,1)} %get-tuple-element.34) | copy-start | bytes 1597444
  94.8 24.7 %copy-start.7 = (bf16[1024,2,128]{2,0,1:T(8,128)(2,1)S(1)}, bf16[1024,2,128]{2,0,1:T(8,128)(2,1)}, u32[]{:S(2)}) copy-start(bf16[1024,2,128]{2,0,1:T(8,128)(2,1)} %copy-done.6) | copy-start | bytes 1572868
  94.8 24.7 %copy-start.17 = (bf16[16,2,128]{2,0,1:T(8,128)(2,1)S(1)}, bf16[16,2,128]{2,0,1:T(8,128)(2,1)}, u32[]{:S(2)}) copy-start(bf16[16,2,128]{2,0,1:T(8,128)(2,1)} %fusion.115) | copy-start | bytes 24580
  117.5 16.0 %collective-permute-start.8 = (bf16[2,256,512]{1,2,0:T(8,128)(2,1)S(1)}, bf16[2,256,512]{1,2,0:T(8,128)(2,1)S(1)}, u32[]{:S(2)}, u32[]{:S(2)}) collective-permute-start(bf16[2,256,512]{1,2,0:T(8,128)(2,1)S(1)} %pad_maximum_fusion.6), channel_id=1, source_target_pairs={{0,32},{4,36},{8,40},{12,44},{16,48},{20,52},{24,56},{28,60},{32,6... | collective-permute-start | bytes 1572872 | tf_op jit(solution)/shard_map/ppermute | solution.py:19
  125.4 56.7 %copy-start.10 = (bf16[1024,1,2,128]{3,0,2,1:T(8,128)(2,1)S(1)}, bf16[1024,1,2,128]{3,0,2,1:T(8,128)(2,1)}, u32[]{:S(2)}) copy-start(bf16[1024,1,2,128]{3,0,2,1:T(8,128)(2,1)} %copy-done.9) | copy-start | bytes 1572868
  125.4 56.7 %copy-start.18 = (bf16[16,2,128]{2,0,1:T(8,128)(2,1)S(1)}, bf16[16,2,128]{2,0,1:T(8,128)(2,1)}, u32[]{:S(2)}) copy-start(bf16[16,2,128]{2,0,1:T(8,128)(2,1)} %copy.104) | copy-start | bytes 24580
  135.2 56.5 %collective-permute-start.9 = (bf16[2,128,512]{1,2,0:T(8,128)(2,1)}, bf16[2,128,512]{1,2,0:T(8,128)(2,1)}, u32[]{:S(2)}, u32[]{:S(2)}) collective-permute-start(bf16[2,128,512]{1,2,0:T(8,128)(2,1)} %pad_maximum_fusion.17), channel_id=1, source_target_pairs={{0,4},{4,8},{8,12},{12,16},{16,20},{20,24},{24,28},{28,32},{32,36}... | collective-permute-start | bytes 786440 | tf_op jit(solution)/shard_map/ppermute | solution.py:19
  137.8 53.8 %collective-permute-start.10 = (bf16[2,256,256]{1,2,0:T(8,128)(2,1)}, bf16[2,256,256]{1,2,0:T(8,128)(2,1)}, u32[]{:S(2)}, u32[]{:S(2)}) collective-permute-start(bf16[2,256,256]{1,2,0:T(8,128)(2,1)} %pad_maximum_fusion.18), channel_id=1, source_target_pairs={{0,68},{4,72},{8,76},{12,80},{16,84},{20,88},{24,92},{28,96},{32,1... | collective-permute-start | bytes 786440 | tf_op jit(solution)/shard_map/ppermute | solution.py:19
  195.7 7.6 %collective-permute-start.11 = (bf16[512,256]{0,1:T(8,128)(2,1)S(1)}, bf16[512,256]{0,1:T(8,128)(2,1)S(1)}, u32[]{:S(2)}, u32[]{:S(2)}) collective-permute-start(bf16[512,256]{0,1:T(8,128)(2,1)S(1)} %convolution_convert_fusion.7), channel_id=1, source_target_pairs={{0,2},{1,3},{2,1},{3,0},{4,6},{5,7},{6,5},{7,4},{8,10},{9,11},{10,... | collective-permute-start | bytes 786440 | tf_op jit(solution)/shard_map/ppermute | solution.py:106
  199.0 16.9 %collective-permute-start.13 = (bf16[512,256]{0,1:T(8,128)(2,1)S(1)}, bf16[512,256]{0,1:T(8,128)(2,1)S(1)}, u32[]{:S(2)}, u32[]{:S(2)}) collective-permute-start(bf16[512,256]{0,1:T(8,128)(2,1)S(1)} %convolution_convert_fusion.6), channel_id=1, source_target_pairs={{0,3},{1,2},{2,0},{3,1},{4,7},{5,6},{6,4},{7,5},{8,11},{9,10},{10,... | collective-permute-start | bytes 786440 | tf_op jit(solution)/shard_map/ppermute | solution.py:109
  203.4 22.2 %collective-permute-start.12 = (bf16[1024,256]{0,1:T(8,128)(2,1)S(1)}, bf16[1024,256]{0,1:T(8,128)(2,1)}, u32[]{:S(2)}, u32[]{:S(2)}) collective-permute-start(bf16[1024,256]{0,1:T(8,128)(2,1)S(1)} %pad_maximum_fusion.7), channel_id=1, source_target_pairs={{0,2},{1,3},{2,1},{3,0},{4,6},{5,7},{6,5},{7,4},{8,10},{9,11},{10,... | collective-permute-start | bytes 1572872 | tf_op jit(solution)/shard_map/ppermute | solution.py:120
  216.9 13.4 %collective-permute-start.14 = (bf16[1024,256]{0,1:T(8,128)(2,1)}, bf16[1024,256]{0,1:T(8,128)(2,1)}, u32[]{:S(2)}, u32[]{:S(2)}) collective-permute-start(bf16[1024,256]{0,1:T(8,128)(2,1)} %pad_maximum_fusion.8), channel_id=1, source_target_pairs={{0,3},{1,2},{2,0},{3,1},{4,7},{5,6},{6,4},{7,5},{8,11},{9,10},{10,... | collective-permute-start | bytes 1572872 | tf_op jit(solution)/shard_map/ppermute | solution.py:121
  217.3 18.5 %copy-start.2 = (bf16[1024,704]{0,1:T(8,128)(2,1)S(1)}, bf16[1024,704]{0,1:T(8,128)(2,1)}, u32[]{:S(2)}) copy-start(bf16[1024,704]{0,1:T(8,128)(2,1)} %param.20) | copy-start | bytes 4325380
  231.9 12.3 %collective-permute-start.16 = (bf16[1024,256]{0,1:T(8,128)(2,1)S(1)}, bf16[1024,256]{0,1:T(8,128)(2,1)S(1)}, u32[]{:S(2)}, u32[]{:S(2)}) collective-permute-start(bf16[1024,256]{0,1:T(8,128)(2,1)S(1)} %get-tuple-element.10), channel_id=1, source_target_pairs={{0,3},{1,2},{2,0},{3,1},{4,7},{5,6},{6,4},{7,5},{8,11},{9,10},{10,... | collective-permute-start | bytes 1572872 | tf_op jit(solution)/shard_map/ppermute | solution.py:72
  232.0 12.3 %collective-permute-start.15 = (bf16[1024,256]{0,1:T(8,128)(2,1)S(1)}, bf16[1024,256]{0,1:T(8,128)(2,1)S(1)}, u32[]{:S(2)}, u32[]{:S(2)}) collective-permute-start(bf16[1024,256]{0,1:T(8,128)(2,1)S(1)} %get-tuple-element.10), channel_id=1, source_target_pairs={{0,2},{1,3},{2,1},{3,0},{4,6},{5,7},{6,5},{7,4},{8,10},{9,11},{10,... | collective-permute-start | bytes 1572872 | tf_op jit(solution)/shard_map/ppermute | solution.py:71
  244.2 7.7 %collective-permute-start.18 = (bf16[512,256]{0,1:T(8,128)(2,1)S(1)}, bf16[512,256]{0,1:T(8,128)(2,1)S(1)}, u32[]{:S(2)}, u32[]{:S(2)}) collective-permute-start(bf16[512,256]{0,1:T(8,128)(2,1)S(1)} %slice.299), channel_id=1, source_target_pairs={{0,3},{1,2},{2,0},{3,1},{4,7},{5,6},{6,4},{7,5},{8,11},{9,10},{10,... | collective-permute-start | bytes 786440 | tf_op jit(solution)/shard_map/ppermute | solution.py:74
  244.4 7.2 %collective-permute-start.17 = (bf16[512,256]{0,1:T(8,128)(2,1)S(1)}, bf16[512,256]{0,1:T(8,128)(2,1)S(1)}, u32[]{:S(2)}, u32[]{:S(2)}) collective-permute-start(bf16[512,256]{0,1:T(8,128)(2,1)S(1)} %slice.298), channel_id=1, source_target_pairs={{0,2},{1,3},{2,1},{3,0},{4,6},{5,7},{6,5},{7,4},{8,10},{9,11},{10,... | collective-permute-start | bytes 786440 | tf_op jit(solution)/shard_map/ppermute | solution.py:73
  255.8 9.8 %collective-permute-start.19 = (bf16[512,256]{0,1:T(8,128)(2,1)S(1)}, bf16[512,256]{0,1:T(8,128)(2,1)S(1)}, u32[]{:S(2)}, u32[]{:S(2)}) collective-permute-start(bf16[512,256]{0,1:T(8,128)(2,1)S(1)} %convolution_convert_fusion.9), channel_id=1, source_target_pairs={{0,2},{1,3},{2,1},{3,0},{4,6},{5,7},{6,5},{7,4},{8,10},{9,11},{10,... | collective-permute-start | bytes 786440 | tf_op jit(solution)/shard_map/ppermute | solution.py:106
  259.5 10.0 %collective-permute-start.21 = (bf16[512,256]{0,1:T(8,128)(2,1)S(1)}, bf16[512,256]{0,1:T(8,128)(2,1)S(1)}, u32[]{:S(2)}, u32[]{:S(2)}) collective-permute-start(bf16[512,256]{0,1:T(8,128)(2,1)S(1)} %convolution_convert_fusion.8), channel_id=1, source_target_pairs={{0,3},{1,2},{2,0},{3,1},{4,7},{5,6},{6,4},{7,5},{8,11},{9,10},{10,... | collective-permute-start | bytes 786440 | tf_op jit(solution)/shard_map/ppermute | solution.py:109
  265.7 10.5 %collective-permute-start.20 = (bf16[1024,256]{0,1:T(8,128)(2,1)S(1)}, bf16[1024,256]{0,1:T(8,128)(2,1)S(1)}, u32[]{:S(2)}, u32[]{:S(2)}) collective-permute-start(bf16[1024,256]{0,1:T(8,128)(2,1)S(1)} %pad_maximum_fusion.9), channel_id=1, source_target_pairs={{0,2},{1,3},{2,1},{3,0},{4,6},{5,7},{6,5},{7,4},{8,10},{9,11},{10,... | collective-permute-start | bytes 1572872 | tf_op jit(solution)/shard_map/ppermute | solution.py:120
  269.6 10.5 %collective-permute-start.22 = (bf16[1024,256]{0,1:T(8,128)(2,1)S(1)}, bf16[1024,256]{0,1:T(8,128)(2,1)S(1)}, u32[]{:S(2)}, u32[]{:S(2)}) collective-permute-start(bf16[1024,256]{0,1:T(8,128)(2,1)S(1)} %pad_maximum_fusion.10), channel_id=1, source_target_pairs={{0,3},{1,2},{2,0},{3,1},{4,7},{5,6},{6,4},{7,5},{8,11},{9,10},{10,... | collective-permute-start | bytes 1572872 | tf_op jit(solution)/shard_map/ppermute | solution.py:121
  (15 other events, 65.4 us)
